TPU v7x, 32 devices: a whole 2x2x4 slice. The times are simulated.
32 devices in a mesh: pair: 4 (over z), gen: 8 (over y, x, core).
Axes of the slice: x: 2, y: 2, z: 4, core: 2. Of those that a mesh axis runs over, the one named last changes fastest.
Arguments:
- tokens: bfloat16 [32768, 2048], P(('pair', 'gen')), may hold values from -6 to 6
- cotangent: bfloat16 [32768, 256], P(('pair', 'gen')), may hold values from -6 to 6
- block_pair: int32 [32, 1], replicated, may hold values from 0 to 15
- src_lang: int32 [16], replicated, may hold values from 0 to 95
- tgt_lang: int32 [16], replicated, may hold values from 0 to 95
- lang_embed: float32 [96, 512], P(None, 'pair'), may hold values from -5 to 5
- generator: bfloat16 [512, 524288], P('pair', 'gen'), may hold values from -0.005859375 to 0.005859375
Outputs:
- grad_tokens: bfloat16 [32768, 2048], P(('pair', 'gen'))
- grad_generator: bfloat16 [512, 524288], P('pair', 'gen')
- grad_embed: float32 [96, 512], P(None, 'pair')
Inputs may be any that keep to these rules, and one draw needn't show every extreme that they name: `block_pair`: every pair owns at least one block; block counts per pair are uneven.
All inputs are finite; a program needn't handle non-finite values.
Results may differ from a plain program's by a relative error of at most 0.007.
Values may be sent and summed in bfloat16 or wider, within the bound.
No kernel may reach another device: no remote copies, remote signals or barrier semaphores. Data moves between devices by JAX's collectives and lax.ppermute only.
A program may use at most 128 MiB of HBM per device.

v0:
```python
import jax
import jax.numpy as jnp
from jax import lax
from jax.sharding import PartitionSpec as P

BLK = 1024


def shards(tokens, cotangent, block_pair, src_lang, tgt_lang, lang_embed, generator):
    gen_count = lax.axis_size("gen")
    pair_index = lax.axis_index("pair")
    blocks_here = tokens.shape[0] // BLK
    model_width = tokens.shape[1]
    adapter_rank = cotangent.shape[1]
    languages = lang_embed.shape[0]
    pair_count = src_lang.shape[0]
    lang_ids = jnp.arange(languages, dtype=jnp.int32)
    hot_both = (src_lang[:, None] == lang_ids[None, :]).astype(jnp.float32) + (
        tgt_lang[:, None] == lang_ids[None, :]
    ).astype(jnp.float32)
    pair_embed = jnp.dot(hot_both, lang_embed, precision=lax.Precision.HIGHEST).astype(jnp.bfloat16)
    partial_value = jnp.dot(pair_embed, generator, preferred_element_type=jnp.float32)
    adapter_cols = lax.psum(partial_value, "pair").astype(jnp.bfloat16)
    flat_pairs = block_pair[:, 0]
    row_pairs = lax.dynamic_slice_in_dim(
        flat_pairs, pair_index * (gen_count * blocks_here), gen_count * blocks_here
    )
    send_order = row_pairs.reshape(gen_count, blocks_here).T
    outgoing = jnp.take(adapter_cols, send_order, axis=0).reshape(
        blocks_here, gen_count * adapter_cols.shape[1]
    )
    own_adapters = lax.all_to_all(outgoing, "gen", split_axis=1, concat_axis=1, tiled=True)
    adapters = own_adapters.reshape(blocks_here, model_width, adapter_rank)
    token_blocks = tokens.reshape(blocks_here, BLK, model_width)
    cot_blocks = cotangent.reshape(blocks_here, BLK, adapter_rank)
    hidden = jnp.einsum("btd,bdr->btr", token_blocks, adapters, preferred_element_type=jnp.float32)
    logistic = jax.nn.sigmoid(hidden)
    grad_hidden = (
        cot_blocks.astype(jnp.float32) * logistic * (1.0 + hidden * (1.0 - logistic))
    ).astype(jnp.bfloat16)
    grad_tokens = (
        jnp.einsum("btr,bdr->btd", grad_hidden, adapters, preferred_element_type=jnp.float32)
        .astype(jnp.bfloat16)
        .reshape(tokens.shape)
    )
    outer_grads = jnp.einsum(
        "btd,btr->bdr", token_blocks, grad_hidden, preferred_element_type=jnp.float32
    ).reshape(blocks_here, model_width * adapter_rank)
    returned = lax.all_to_all(outer_grads, "gen", split_axis=1, concat_axis=0, tiled=True)
    pair_ids = jnp.arange(pair_count, dtype=jnp.int32)
    segment_hot = (pair_ids[:, None] == row_pairs[None, :]).astype(jnp.float32)
    row_grad = jnp.dot(segment_hot, returned, precision=lax.Precision.HIGHEST)
    grad_rounded = lax.psum(row_grad, "pair").astype(jnp.bfloat16)
    grad_generator = jnp.einsum(
        "pe,pc->ec", pair_embed, grad_rounded, preferred_element_type=jnp.float32
    ).astype(jnp.bfloat16)
    partial_pair = jnp.einsum(
        "pc,ec->pe", grad_rounded, generator, preferred_element_type=jnp.float32
    )
    grad_pair = lax.psum(partial_pair, "gen")
    grad_embed = jnp.dot(hot_both.T, grad_pair, precision=lax.Precision.HIGHEST)
    return (grad_tokens, grad_generator, grad_embed)


def solution(mesh):
    placed = (
        P(("pair", "gen"), None),
        P(("pair", "gen"), None),
        P(),
        P(),
        P(),
        P(None, "pair"),
        P("pair", "gen"),
    )
    return jax.shard_map(
        shards,
        mesh=mesh,
        in_specs=placed,
        out_specs=(P(("pair", "gen"), None), P("pair", "gen"), P(None, "pair")),
        check_vma=False,
    )
```

profile of v0, /device:TPU:0, one launch (start us, length us, event | category | flops | bytes accessed | tf_op | source)
XLA Modules:
  0.0 421.6 jit_solution(15591775119214140472)
XLA Ops:
  0.6 0.0 copy-start
  0.7 0.7 fusion.16
  1.4 0.7 compare_and_fusion
  2.1 0.9 convolution_convert_fusion.2
  3.0 10.1 %fusion.21 = f32[16,65536]{1,0:T(8,128)} fusion(bf16[16,128]{1,0:T(8,128)(2,1)S(1)} %convolution_convert_fusion.2, bf16[128,65536]{1,0:T(8,128)(2,1)} %param.13), kind=kOutput, calls=%fused_computation.39 | convolution fusion | flops 268435456 | bytes 20975616 | tf_op jit(solution)/shard_map/dot_general | solution.py:22
  13.1 149.0 %all-reduce.2 = bf16[16,65536]{1,0:T(8,128)(2,1)S(1)} all-reduce(f32[16,65536]{1,0:T(8,128)} %fusion.21), channel_id=1, replica_groups=mesh['pair'=4,'gen'=8] {'pair'}, use_global_device_ids=true, to_apply=%region_0.0 | all-reduce | flops 1048576 | bytes 6291456 | tf_op jit(solution)/shard_map/psum | solution.py:23
  162.1 1.2 gather_fusion
  163.4 0.2 bitcast_select_fusion
  163.5 1.6 copy.27
  165.2 0.5 broadcast.100
  165.7 7.0 %reduce.2 = bf16[8,65536]{1,0:T(8,128)(2,1)S(1)} reduce(bf16[8,1,65536]{2,1,0:T(2,128)(2,1)S(1)} %bitcast.33, bf16[]{:T(256)} %broadcast.100), dimensions={1}, to_apply=%bitcast.32.reduce_sub_computation | reduce | bytes 2097154
  172.7 1.9 reshape.166
  174.6 3.8 all-to-all-start
  178.4 1.0 copy.17
  179.4 14.3 %all-to-all-done = bf16[8,2,32768]{2,1,0:T(2,128)(2,1)S(1)} async-done(((bf16[8,2,32768]{2,1,0:T(2,128)(2,1)}), bf16[8,2,32768]{2,1,0:T(2,128)(2,1)S(1)}, u32[]{:S(2)}, u32[]{:S(2)}) %all-to-all-start) | async-done | bytes 1048608 | tf_op jit(solution)/shard_map/all_to_all | solution.py:32
  193.7 1.0 reshape.167
  194.8 6.0 %bitcast_reduce_fusion = bf16[8,65536]{1,0:T(8,128)(2,1)S(1)} fusion(bf16[8,1,65536]{2,1,0:T(2,128)(2,1)S(1)} %reshape.167), kind=kLoop, calls=%fused_computation.37 | loop fusion | bytes 2097152 | tf_op jit(solution)/shard_map/all_to_all | solution.py:32
  200.8 0.5 reshape.156
  201.3 3.9 convolution_bitcast_fusion.1
  205.2 1.0 copy-done.9
  206.2 2.9 convolution_bitcast_fusion
  209.1 1.9 copy.19
  211.0 4.2 all_to_all.20
  215.2 3.9 all-to-all-start.1
  219.0 5.0 %convolution_convert_fusion.1 = bf16[1024,2048]{1,0:T(8,128)(2,1)} fusion(bf16[2048,256]{1,0:T(8,128)(2,1)S(1)} %copy-done.3, f32[1024,256]{0,1:T(8,128)} %copy-done.9, bf16[1024,256]{0,1:T(8,128)(2,1)} %copy.17), kind=kOutput, calls=%fused_computation.2 | convolution fusion | flops 1078460416 | bytes 6815744 | tf_op jit(solution)/shard_map/btr,bdr->btd/dot_general | solution.py:42
  224.0 21.3 %all-to-all-done.1 = f32[1,8,65536]{2,0,1:T(1,128)S(1)} async-done(((f32[1,8,65536]{2,0,1:T(1,128)}), f32[1,8,65536]{2,0,1:T(1,128)S(1)}, u32[]{:S(2)}, u32[]{:S(2)}) %all-to-all-start.1) | async-done | bytes 2097184 | tf_op jit(solution)/shard_map/all_to_all | solution.py:49
  245.3 4.8 %fusion = f32[16,65536]{1,0:T(8,128)} fusion(f32[1,8,65536]{2,0,1:T(1,128)S(1)} %all-to-all-done.1, s32[8]{0:T(128)S(1)} %get-tuple-element.4), kind=kOutput, calls=%fused_computation.4 | convolution fusion | flops 100663424 | bytes 6291488 | tf_op jit(solution)/shard_map/dot_general | solution.py:52
  250.1 141.2 %all-reduce.3 = bf16[16,65536]{1,0:T(8,128)(2,1)S(1)} all-reduce(f32[16,65536]{1,0:T(8,128)} %fusion), channel_id=1, replica_groups=mesh['pair'=4,'gen'=8] {'pair'}, use_global_device_ids=true, to_apply=%region_1.2 | all-reduce | flops 1048576 | bytes 6291456 | tf_op jit(solution)/shard_map/psum | solution.py:53
  391.4 8.5 %convolution_convert_fusion = bf16[128,65536]{1,0:T(8,128)(2,1)} fusion(bf16[16,128]{1,0:T(8,128)(2,1)S(1)} %convolution_convert_fusion.2, bf16[16,65536]{1,0:T(8,128)(2,1)S(1)} %all-reduce.3), kind=kOutput, calls=%fused_computation.1 | convolution fusion | flops 276824064 | bytes 18878464 | tf_op jit(solution)/shard_map/pe,pc->ec/dot_general | solution.py:54
  399.9 8.1 %fusion.22 = f32[16,128]{1,0:T(8,128)S(1)} fusion(bf16[16,65536]{1,0:T(8,128)(2,1)S(1)} %all-reduce.3, bf16[128,65536]{1,0:T(8,128)(2,1)} %param.13), kind=kOutput, calls=%fused_computation.40 | convolution fusion | flops 268435456 | bytes 18882560 | tf_op jit(solution)/shard_map/pc,ec->pe/dot_general | solution.py:57
  408.0 12.6 %psum.23 = f32[16,128]{1,0:T(8,128)S(1)} all-reduce(f32[16,128]{1,0:T(8,128)S(1)} %fusion.22), channel_id=1, replica_groups=mesh['pair'=4,'gen'=8] {'gen'}, use_global_device_ids=true, to_apply=%region_2.3 | all-reduce | flops 2048 | bytes 16384 | tf_op jit(solution)/shard_map/psum | solution.py:60
  420.6 1.0 fusion.10
  (19 shorter events, 0.0 us)
Async XLA Ops:
  0.6 1.5 copy-start
  172.7 5.7 %copy-start.4 = (bf16[1024,256]{1,0:T(8,128)(2,1)S(1)}, bf16[1024,256]{1,0:T(8,128)(2,1)}, u32[]{:S(2)}) copy-start(bf16[1024,256]{1,0:T(8,128)(2,1)} %param.8) | copy-start | bytes 1572868
  174.6 19.1 %all-to-all-start = ((bf16[8,2,32768]{2,1,0:T(2,128)(2,1)}), bf16[8,2,32768]{2,1,0:T(2,128)(2,1)S(1)}, u32[]{:S(2)}, u32[]{:S(2)}) async-start(bf16[8,2,32768]{2,1,0:T(2,128)(2,1)} %reshape.166), calls=%async_computation | async-start | bytes 2097152 | tf_op jit(solution)/shard_map/all_to_all | solution.py:32
  201.3 3.9 copy-start.2
  201.3 4.9 %copy-start.5 = (bf16[1024,256]{0,1:T(8,128)(2,1)S(1)}, bf16[1024,256]{0,1:T(8,128)(2,1)}, u32[]{:S(2)}) copy-start(bf16[1024,256]{0,1:T(8,128)(2,1)} %copy.17) | copy-start | bytes 1572868
  201.3 4.9 %copy-start.6 = (bf16[1024,2048]{1,0:T(8,128)(2,1)S(1)}, bf16[1024,2048]{1,0:T(8,128)(2,1)}, u32[]{:S(2)}) copy-start(bf16[1024,2048]{1,0:T(8,128)(2,1)} %param.7) | copy-start | bytes 12582916
  205.2 1.0 copy-start.9
  211.0 8.0 %copy-start.3 = (bf16[2048,256]{1,0:T(8,128)(2,1)S(1)}, bf16[2048,256]{1,0:T(8,128)(2,1)}, u32[]{:S(2)}) copy-start(bf16[2048,256]{1,0:T(8,128)(2,1)} %copy-done.2) | copy-start | bytes 3145732
  215.2 30.2 %all-to-all-start.1 = ((f32[1,8,65536]{2,0,1:T(1,128)}), f32[1,8,65536]{2,0,1:T(1,128)S(1)}, u32[]{:S(2)}, u32[]{:S(2)}) async-start(f32[1,8,65536]{2,0,1:T(1,128)} %all_to_all.20), calls=%async_computation.1 | async-start | bytes 4194304 | tf_op jit(solution)/shard_map/all_to_all | solution.py:49
  399.9 20.7 %copy-start.7 = (s32[16]{0:T(128)S(1)}, s32[16]{0:T(128)}, u32[]{:S(2)}) copy-start(s32[16]{0:T(128)} %param.11) | copy-start | bytes 196
  399.9 20.7 %copy-start.8 = (s32[16]{0:T(128)S(1)}, s32[16]{0:T(128)}, u32[]{:S(2)}) copy-start(s32[16]{0:T(128)} %param.10) | copy-start | bytes 196
  399.9 21.7 %copy-start.1 = (f32[96,128]{1,0:T(8,128)S(1)}, f32[96,128]{1,0:T(8,128)}, u32[]{:S(2)}) copy-start(f32[96,128]{1,0:T(8,128)} %param.12) | copy-start | bytes 147460
where the time goes:
time: 422 us
  blocking collectives  303 us (72%)
  matrix products  45.1 us (11%)
  waiting for transfers between devices  35.7 us (8%)
  local copies, waits for them, and re-layouts  20.8 us (5%)
  other arithmetic  8.67 us (2%)
  starting transfers between devices  7.64 us (2%)
    psum x1, blocking collectives, shards(): adapter_cols = lax.psum(partial_value, 'pair').astype(jnp.bfloat16)  149 us
    psum x1, blocking collectives, shards(): grad_rounded = lax.psum(row_grad, 'pair').astype(jnp.bfloat16)  141 us
    all_to_all x1, waiting for transfers between devices, shards(): lax.all_to_all(outer_grads, 'gen', split_axis=1, concat_axis=0, tiled=True)  21.3 us
    all_to_all x1, waiting for transfers between devices, shards(): lax.all_to_all(outgoing, 'gen', split_axis=1, concat_axis=1, tiled=True)  14.3 us
    psum x1, blocking collectives, shards(): grad_pair = lax.psum(partial_pair, 'gen')  12.6 us
    dot_general x1, matrix products, shards(): jnp.dot(pair_embed, generator, preferred_element_type=jnp.float32)  10.1 us
    dot_general x1, matrix products, shards(): jnp.einsum('pe,pc->ec', pair_embed, grad_rounded, preferred_element_type=...  8.55 us
  transfers between devices with their start and end apart: 2, of which 2 were waited for; matrix products, arithmetic and copies ran while one was open for 1% of the time, Pallas kernels for 0%

commit v1 on v0

--- a/solution.py
+++ b/solution.py
@@ -4,6 +4,12 @@
 from jax.sharding import PartitionSpec as P
 
 BLK = 1024
+
+
+def stacked_exchange(x, mesh_axis, split, join):
+    pieces = jnp.split(x, lax.axis_size(mesh_axis), axis=split)
+    received = lax.all_to_all(jnp.stack(pieces), mesh_axis, 0, 0)
+    return jnp.concatenate(received, axis=join)
 
 
 def shards(tokens, cotangent, block_pair, src_lang, tgt_lang, lang_embed, generator):
@@ -46,7 +52,7 @@
     outer_grads = jnp.einsum(
         "btd,btr->bdr", token_blocks, grad_hidden, preferred_element_type=jnp.float32
     ).reshape(blocks_here, model_width * adapter_rank)
-    returned = lax.all_to_all(outer_grads, "gen", split_axis=1, concat_axis=0, tiled=True)
+    returned = stacked_exchange(outer_grads, "gen", 1, 0)
     pair_ids = jnp.arange(pair_count, dtype=jnp.int32)
     segment_hot = (pair_ids[:, None] == row_pairs[None, :]).astype(jnp.float32)
     row_grad = jnp.dot(segment_hot, returned, precision=lax.Precision.HIGHEST)

time: 422 us -> 432 us (1.024)
  local copies, waits for them, and re-layouts: 20.8 us -> 31 us
    unnamed x24 -> x28, local copies, waits for them, and re-layouts: 5.44 us -> 19.1 us
where the time goes in v1:
time: 432 us
  blocking collectives  303 us (70%)
  matrix products  44.8 us (10%)
  waiting for transfers between devices  35.6 us (8%)
  local copies, waits for them, and re-layouts  31 us (7%)
  other arithmetic  8.67 us (2%)
  starting transfers between devices  7.64 us (2%)
    psum x1, blocking collectives, shards(): adapter_cols = lax.psum(partial_value, 'pair').astype(jnp.bfloat16)  149 us
    psum x1, blocking collectives, shards(): grad_rounded = lax.psum(row_grad, 'pair').astype(jnp.bfloat16)  142 us
    all_to_all x1, waiting for transfers between devices, stacked_exchange(): received = lax.all_to_all(jnp.stack(pieces), mesh_axis, 0, 0)  21.3 us
    unnamed x28, local copies, waits for them, and re-layouts  19.1 us
    all_to_all x1, waiting for transfers between devices, shards(): lax.all_to_all(outgoing, 'gen', split_axis=1, concat_axis=1, tiled=True)  14.3 us
    psum x1, blocking collectives, shards(): grad_pair = lax.psum(partial_pair, 'gen')  12 us
    dot_general x1, matrix products, shards(): jnp.dot(pair_embed, generator, preferred_element_type=jnp.float32)  10.1 us
  transfers between devices with their start and end apart: 2, of which 2 were waited for; matrix products, arithmetic and copies ran while one was open for 1% of the time, Pallas kernels for 0%

profile of v1, /device:TPU:0, one launch (start us, length us, event | category | flops | bytes accessed | tf_op | source)
XLA Modules:
  0.0 431.7 jit_solution(16448050527717580973)
XLA Ops:
  0.7 0.7 fusion.24
  1.4 0.7 compare_and_fusion
  2.1 0.9 convolution_convert_fusion.2
  3.0 10.1 %fusion.29 = f32[16,65536]{1,0:T(8,128)} fusion(bf16[16,128]{1,0:T(8,128)(2,1)S(1)} %convolution_convert_fusion.2, bf16[128,65536]{1,0:T(8,128)(2,1)} %param.13), kind=kOutput, calls=%fused_computation.55 | convolution fusion | flops 268435456 | bytes 20975616 | tf_op jit(solution)/shard_map/dot_general | solution.py:28
  13.1 149.0 %all-reduce.2 = bf16[16,65536]{1,0:T(8,128)(2,1)S(1)} all-reduce(f32[16,65536]{1,0:T(8,128)} %fusion.29), channel_id=1, replica_groups=mesh['pair'=4,'gen'=8] {'pair'}, use_global_device_ids=true, to_apply=%region_0.0 | all-reduce | flops 1048576 | bytes 6291456 | tf_op jit(solution)/shard_map/psum | solution.py:29
  162.1 1.2 gather_fusion
  163.5 1.6 copy.26
  165.7 7.0 %reduce.2 = bf16[8,65536]{1,0:T(8,128)(2,1)S(1)} reduce(bf16[8,1,65536]{2,1,0:T(2,128)(2,1)S(1)} %bitcast.76, bf16[]{:T(256)} %broadcast.100), dimensions={1}, to_apply=%bitcast.67.reduce_sub_computation | reduce | bytes 2097154
  172.7 1.9 reshape.166
  174.6 3.8 all-to-all-start
  178.4 1.0 copy.16
  179.4 14.3 %all-to-all-done = bf16[8,2,32768]{2,1,0:T(2,128)(2,1)S(1)} async-done(((bf16[8,2,32768]{2,1,0:T(2,128)(2,1)}), bf16[8,2,32768]{2,1,0:T(2,128)(2,1)S(1)}, u32[]{:S(2)}, u32[]{:S(2)}) %all-to-all-start) | async-done | bytes 1048608 | tf_op jit(solution)/shard_map/all_to_all | solution.py:38
  193.7 1.0 reshape.167
  194.8 6.0 %bitcast_reduce_fusion = bf16[8,65536]{1,0:T(8,128)(2,1)S(1)} fusion(bf16[8,1,65536]{2,1,0:T(2,128)(2,1)S(1)} %reshape.167), kind=kLoop, calls=%fused_computation.53 | loop fusion | bytes 2097152 | tf_op jit(solution)/shard_map/all_to_all | solution.py:38
  201.3 3.6 convolution_bitcast_fusion.1
  204.9 1.0 copy-done.7
  205.9 2.8 convolution_bitcast_fusion
  208.7 1.9 copy.18
  210.7 8.6 %copy.20 = f32[1,1,2048,256]{3,1,2,0:T(1,128)S(1)} copy(f32[1,1,2048,256]{3,2,1,0:T(8,128)S(1)} %bitcast.77) | data formatting | bytes 4194304
  219.2 0.7 fusion.17
  220.0 0.7 fusion.16
  220.7 0.7 fusion.15
  221.4 0.7 fusion.14
  225.0 3.9 all-to-all-start.1
  228.9 5.0 %convolution_convert_fusion.1 = bf16[1024,2048]{1,0:T(8,128)(2,1)} fusion(bf16[2048,256]{1,0:T(8,128)(2,1)S(1)} %reshape.154, f32[1024,256]{0,1:T(8,128)} %copy-done.7, bf16[1024,256]{0,1:T(8,128)(2,1)} %copy.16), kind=kOutput, calls=%fused_computation.2 | convolution fusion | flops 1078460416 | bytes 6815744 | tf_op jit(solution)/shard_map/btr,bdr->btd/dot_general | solution.py:48
  233.9 21.3 %all-to-all-done.1 = f32[8,1,65536]{2,1,0:T(1,128)S(1)} async-done(((f32[8,1,65536]{2,1,0:T(1,128)}), f32[8,1,65536]{2,1,0:T(1,128)S(1)}, u32[]{:S(2)}, u32[]{:S(2)}) %all-to-all-start.1) | async-done | bytes 2097184 | tf_op jit(solution)/shard_map/all_to_all | solution.py:11
  255.2 4.8 %fusion = f32[16,65536]{1,0:T(8,128)} fusion(f32[8,1,65536]{2,1,0:T(1,128)S(1)} %all-to-all-done.1, s32[8]{0:T(128)S(1)} %get-tuple-element.4), kind=kOutput, calls=%fused_computation.4 | convolution fusion | flops 100663424 | bytes 6291488 | tf_op jit(solution)/shard_map/dot_general | solution.py:58
  260.0 142.1 %all-reduce.3 = bf16[16,65536]{1,0:T(8,128)(2,1)S(1)} all-reduce(f32[16,65536]{1,0:T(8,128)} %fusion), channel_id=1, replica_groups=mesh['pair'=4,'gen'=8] {'pair'}, use_global_device_ids=true, to_apply=%region_1.2 | all-reduce | flops 1048576 | bytes 6291456 | tf_op jit(solution)/shard_map/psum | solution.py:59
  402.1 8.5 %convolution_convert_fusion = bf16[128,65536]{1,0:T(8,128)(2,1)} fusion(bf16[16,128]{1,0:T(8,128)(2,1)S(1)} %convolution_convert_fusion.2, bf16[16,65536]{1,0:T(8,128)(2,1)S(1)} %all-reduce.3), kind=kOutput, calls=%fused_computation.1 | convolution fusion | flops 276824064 | bytes 18878464 | tf_op jit(solution)/shard_map/pe,pc->ec/dot_general | solution.py:60
  410.6 8.1 %fusion.30 = f32[16,128]{1,0:T(8,128)S(1)} fusion(bf16[16,65536]{1,0:T(8,128)(2,1)S(1)} %all-reduce.3, bf16[128,65536]{1,0:T(8,128)(2,1)} %param.13), kind=kOutput, calls=%fused_computation.56 | convolution fusion | flops 268435456 | bytes 18882560 | tf_op jit(solution)/shard_map/pc,ec->pe/dot_general | solution.py:63
  418.7 12.0 %psum.23 = f32[16,128]{1,0:T(8,128)S(1)} all-reduce(f32[16,128]{1,0:T(8,128)S(1)} %fusion.30), channel_id=1, replica_groups=mesh['pair'=4,'gen'=8] {'gen'}, use_global_device_ids=true, to_apply=%region_2.3 | all-reduce | flops 2048 | bytes 16384 | tf_op jit(solution)/shard_map/psum | solution.py:66
  430.8 1.0 fusion.18
  (23 shorter events, 4.1 us)
Async XLA Ops:
  0.6 1.5 copy-start
  172.7 5.7 %copy-start.2 = (bf16[1024,256]{1,0:T(8,128)(2,1)S(1)}, bf16[1024,256]{1,0:T(8,128)(2,1)}, u32[]{:S(2)}) copy-start(bf16[1024,256]{1,0:T(8,128)(2,1)} %param.8) | copy-start | bytes 1572868
  174.6 19.1 %all-to-all-start = ((bf16[8,2,32768]{2,1,0:T(2,128)(2,1)}), bf16[8,2,32768]{2,1,0:T(2,128)(2,1)S(1)}, u32[]{:S(2)}, u32[]{:S(2)}) async-start(bf16[8,2,32768]{2,1,0:T(2,128)(2,1)} %reshape.166), calls=%async_computation | async-start | bytes 2097152 | tf_op jit(solution)/shard_map/all_to_all | solution.py:38
  201.3 4.7 %copy-start.3 = (bf16[1024,256]{0,1:T(8,128)(2,1)S(1)}, bf16[1024,256]{0,1:T(8,128)(2,1)}, u32[]{:S(2)}) copy-start(bf16[1024,256]{0,1:T(8,128)(2,1)} %copy.16) | copy-start | bytes 1572868
  201.3 4.6 %copy-start.4 = (bf16[1024,2048]{1,0:T(8,128)(2,1)S(1)}, bf16[1024,2048]{1,0:T(8,128)(2,1)}, u32[]{:S(2)}) copy-start(bf16[1024,2048]{1,0:T(8,128)(2,1)} %param.7) | copy-start | bytes 12582916
  204.9 1.0 copy-start.7
  225.0 30.2 %all-to-all-start.1 = ((f32[8,1,65536]{2,1,0:T(1,128)}), f32[8,1,65536]{2,1,0:T(1,128)S(1)}, u32[]{:S(2)}, u32[]{:S(2)}) async-start(f32[8,1,65536]{2,1,0:T(1,128)} %fusion.10), calls=%async_computation.1 | async-start | bytes 4194304 | tf_op jit(solution)/shard_map/all_to_all | solution.py:11
  410.6 20.1 %copy-start.5 = (s32[16]{0:T(128)S(1)}, s32[16]{0:T(128)}, u32[]{:S(2)}) copy-start(s32[16]{0:T(128)} %param.11) | copy-start | bytes 196
  410.6 20.1 %copy-start.6 = (s32[16]{0:T(128)S(1)}, s32[16]{0:T(128)}, u32[]{:S(2)}) copy-start(s32[16]{0:T(128)} %param.10) | copy-start | bytes 196
  410.6 21.1 %copy-start.1 = (f32[96,128]{1,0:T(8,128)S(1)}, f32[96,128]{1,0:T(8,128)}, u32[]{:S(2)}) copy-start(f32[96,128]{1,0:T(8,128)} %param.12) | copy-start | bytes 147460
